TPU v7x, 256 devices: a whole 4x4x8 slice. The times are simulated.
256 devices in a mesh: rep: 64 (over y, x, z_lo), slab: 4 (over z_hi, core).
Axes of the slice: x: 4, y: 4, z: 8 (z_hi: 2, z_lo: 4; z = z_hi * 4 + z_lo), core: 2. Of those that a mesh axis runs over, the one named last changes fastest.
Arguments:
- positions: float32 [64, 3, 16384], P('rep', None, 'slab'), may hold values from 0 to 2
- velocities: float32 [64, 3, 16384], P('rep', None, 'slab'), may hold values from -6 to 6
- inv_mass: float32 [16384], P('slab'), may hold values from 0.5 to 2
- strength: float32 [16384], P('slab'), may hold values from 0.5 to 2
- charge: float32 [16384], P('slab'), may hold values from -1 to 1
- scaling: float32 [64], P('rep'), may hold values from 0.3 to 1
- tile_pairs: int32 [64, 2, 768], P('rep', None, 'slab'), may hold values from 0 to 79, as said below
- tile_counts: int32 [64, 4], P('rep', 'slab'), may hold values from 24 to 192, as said below
- halo_clusters: int32 [64, 64], P('rep', 'slab'), may hold values from 0 to 63, as said below
- swap_pairs: int32 [16, 2], replicated, may hold values from 0 to 63, as said below
Outputs:
- new_positions: float32 [64, 3, 16384], P('rep', None, 'slab')
- new_velocities: float32 [64, 3, 16384], P('rep', None, 'slab')
- potential: float32 [64], P('rep')
Inputs may be any that keep to these rules, and one draw needn't show every extreme that they name: `tile_pairs`: for each replica and slab, the 192 columns are distinct tiles (i, j) with i a cluster of that slab and i <= j; j below 64 is a cluster of the same slab, j = 64 + h is halo slot h. Only the first tile_counts columns are live. `tile_counts`: in every replica some slab has all 192 tiles live. `halo_clusters`: the 16 clusters of each replica and slab are distinct. `swap_pairs`: no replica appears twice. The first pair joins two replicas 64 // 2 apart (counted round), the second two neighbouring replicas (counted round); the others are arbitrary.
All inputs are finite; a program needn't handle non-finite values.
Results may differ from a plain program's by a relative error of at most 0.0003.
Values sent between devices are 32-bit elements; how exact they have to be, the bound alone decides.
No kernel may reach another device: no remote copies, remote signals or barrier semaphores. Data moves between devices by JAX's collectives and lax.ppermute only.
A program may use at most 64 MiB of HBM per device.

v0:
```python
import jax
import jax.numpy as jnp
from jax import lax
from jax.sharding import PartitionSpec as P

CL = 64
CD = 64
STEPS = 4
HALO = 16
NT_MAX = 192
tile_block = 16
time_step = 0.04
half_step = 0.02
soft_sq = 0.25
slab_width = 2.0
exact = lax.Precision.HIGHEST


def from_behind(value, axis, steps):
    count = lax.axis_size(axis)
    pairs = [(source, (source + steps) % count) for source in range(count)]
    return lax.ppermute(value, axis, pairs)


def partner_of(pair_list, replica_ids):
    first_col = pair_list[:, 0]
    second_col = pair_list[:, 1]
    hit_first = replica_ids[:, None] == first_col[None, :]
    hit_second = replica_ids[:, None] == second_col[None, :]
    partner_sum = jnp.sum(jnp.where(hit_first, second_col[None, :], 0), 1) + jnp.sum(
        jnp.where(hit_second, first_col[None, :], 0), 1
    )
    listed = jnp.any(hit_first, 1) | jnp.any(hit_second, 1)
    return jnp.where(listed, partner_sum, replica_ids)


def select_table(index_list, width):
    cluster_ids = jnp.arange(width, dtype=jnp.int32)
    return (index_list[:, None] == cluster_ids[None, :]).astype(jnp.float32)


def pair_block(extended, strength_all, charge_all, ham_scale, tile_first, tile_second, live_mask):
    count_tiles = tile_first.shape[0]
    width = extended.shape[1]
    select_first = select_table(tile_first, width)
    select_second = select_table(tile_second, width)
    coords_i = jnp.einsum("te,xec->xct", select_first, extended, precision=exact)
    coords_j = jnp.einsum("te,xec->xtc", select_second, extended, precision=exact)
    offsets = (coords_i[:, :, :, None] - coords_j[:, None, :, :]).reshape(3, CL, count_tiles * CL)
    sq_dist = offsets[0] * offsets[0] + offsets[1] * offsets[1] + offsets[2] * offsets[2]
    params_all = jnp.stack([strength_all, charge_all], 0)
    params_i = jnp.einsum("te,pec->pct", select_first, params_all, precision=exact)
    params_j = jnp.einsum("te,pec->ptc", select_second, params_all, precision=exact)
    strength_prod = (params_i[0][:, :, None] * params_j[0][None, :, :]).reshape(
        CL, count_tiles * CL
    )
    charge_prod = (params_i[1][:, :, None] * params_j[1][None, :, :]).reshape(CL, count_tiles * CL)
    gauss_term = strength_prod * jnp.exp(-sq_dist)
    inv_root = lax.rsqrt(sq_dist + soft_sq)
    coulomb = ham_scale * charge_prod * inv_root
    same_tile = tile_first == tile_second
    weight_tile = jnp.where(live_mask, jnp.where(same_tile, 0.5, 1.0), 0.0).astype(jnp.float32)
    weight_col = jnp.repeat(weight_tile, CL)[None, :]
    slope = gauss_term + 0.5 * coulomb * inv_root * inv_root
    pushes = (2.0 * slope * weight_col)[None, :, :] * offsets
    force_i = pushes.reshape(3, CL, count_tiles, CL).sum(-1)
    force_j = -pushes.sum(1).reshape(3, count_tiles, CL)
    atom_ids = jnp.arange(CL, dtype=jnp.int32)
    column_ids = jnp.arange(count_tiles * CL, dtype=jnp.int32) % CL
    self_pair = jnp.repeat(same_tile, CL)[None, :] & (atom_ids[:, None] == column_ids[None, :])
    energy = jnp.sum(jnp.where(self_pair, 0.0, (gauss_term + coulomb) * weight_col))
    spread_i = jnp.einsum("te,xct->xec", select_first, force_i, precision=exact)
    spread_j = jnp.einsum("te,xtc->xec", select_second, force_j, precision=exact)
    return (spread_i + spread_j, energy)


def local(
    positions,
    velocities,
    inv_mass,
    strength,
    charge,
    scaling,
    tile_pairs,
    tile_counts,
    halo_clusters,
    swap_pairs,
):
    coords = positions[0]
    speeds = velocities[0]
    ham_scale = scaling[0]
    firsts_flat = tile_pairs[0, 0]
    seconds_flat = tile_pairs[0, 1]
    live_count = tile_counts[0, 0]
    halo_index = halo_clusters[0]
    atoms_here = coords.shape[1]
    halo_table = select_table(halo_index, CD)
    params = jnp.stack([strength, charge], 0).reshape(2, CD, CL)
    sent_params = jnp.einsum("hc,pck->phk", halo_table, params, precision=exact).reshape(
        2, HALO * CL
    )
    got_params = from_behind(sent_params, "slab", -1).reshape(2, HALO, CL)
    strength_all = jnp.concatenate([params[0], got_params[0]], 0)
    charge_all = jnp.concatenate([params[1], got_params[1]], 0)
    lift = jnp.array([0.0, 0.0, slab_width], jnp.float32)[:, None]
    extended_now = [None]

    def add_block(totals, tile_first, tile_second, slot_row):
        spread, energy_part = pair_block(
            extended_now[0],
            strength_all,
            charge_all,
            ham_scale,
            tile_first,
            tile_second,
            slot_row < live_count,
        )
        return (totals[0] + spread, totals[1] + energy_part)

    def evaluate(coords_now):
        blocks = coords_now.reshape(3, CD, CL)
        sent_coords = jnp.einsum("hc,xck->xhk", halo_table, blocks, precision=exact).reshape(
            3, HALO * CL
        )
        from_above = from_behind(sent_coords, "slab", -1) + lift
        extended_now[0] = jnp.concatenate([blocks, from_above.reshape(3, HALO, CL)], 1)
        start_state = (jnp.zeros((3, CD + HALO, CL), jnp.float32), jnp.zeros((), jnp.float32))
        firsts = firsts_flat.reshape(-1, tile_block)
        seconds = seconds_flat.reshape(-1, tile_block)
        slot_ids = jnp.arange(NT_MAX, dtype=jnp.int32).reshape(-1, tile_block)

        def visit_block(totals, inputs):
            return (add_block(totals, inputs[0], inputs[1], inputs[2]), None)

        result, _ = lax.scan(visit_block, start_state, (firsts, seconds, slot_ids))
        forces, energy = result
        returned = from_behind(forces[:, CD:].reshape(3, HALO * CL), "slab", 1)
        back_home = jnp.einsum(
            "hc,xhk->xck", halo_table, returned.reshape(3, HALO, CL), precision=exact
        )
        local_forces = forces[:, :CD] + back_home
        return (local_forces.reshape(3, atoms_here), energy)

    forces, energy = evaluate(coords)
    for step_idx in range(STEPS):
        speeds = speeds + half_step * forces * inv_mass
        coords = coords + time_step * speeds
        forces, energy = evaluate(coords)
        speeds = speeds + half_step * forces * inv_mass
    total_energy = lax.psum(energy, "slab")
    potential = (total_energy / (atoms_here * lax.axis_size("slab"))).reshape(1)
    state = jnp.concatenate([coords, speeds], 0)
    partner_me = partner_of(swap_pairs, lax.axis_index("rep").reshape(1))[0]
    shard_rows = lax.all_gather(state[None], "rep", axis=0, tiled=True)
    row_ids = jnp.arange(shard_rows.shape[0], dtype=jnp.int32)
    chosen = row_ids == partner_me
    swapped = jnp.sum(jnp.where(chosen[:, None, None], shard_rows, 0.0), 0)
    return (swapped[:3][None], swapped[3:][None], potential)


def solution(mesh):
    in_specs = (
        P("rep", None, "slab"),
        P("rep", None, "slab"),
        P("slab"),
        P("slab"),
        P("slab"),
        P("rep"),
        P("rep", None, "slab"),
        P("rep", "slab"),
        P("rep", "slab"),
        P(),
    )
    out_specs = (P("rep", None, "slab"), P("rep", None, "slab"), P("rep"))
    return jax.shard_map(local, mesh=mesh, in_specs=in_specs, out_specs=out_specs, check_vma=False)
```

profile of v0, /device:TPU:0, one launch (start us, length us, event | category | flops | bytes accessed | tf_op | source)
XLA Modules:
  0.0 775.9 jit_solution(11839752525932202935)
XLA Ops:
  9.7 4.9 collective-permute-start
  21.1 60.0 %while.67 = (s32[]{:T(128)}, f32[3,80,64]{1,2,0:T(8,128)S(1)}, s32[12,16]{1,0:T(8,128)S(1)}, f32[2,80,64]{1,2,0:T(8,128)S(1)}, s32[12,16]{1,0:T(8,128)S(1)}, /*i...) while((s32[]{:T(128)}, f32[3,80,64]{1,2,0:T(8,128)S(1)}, ...), condition=%wide.region_7.8_spmd.clone, body=%wide.region_4.7_spmd.clone.sunk | while | flops 17876564 | bytes 2778059 | solution.py:135
  23.6 1.0 fusion.306
  28.6 1.0 fusion.306
  33.6 1.0 fusion.306
  38.6 1.0 fusion.306
  43.6 1.0 fusion.306
  48.6 1.0 fusion.306
  53.6 1.0 fusion.306
  58.6 1.0 fusion.306
  63.6 1.0 fusion.306
  68.6 1.0 fusion.306
  73.6 1.0 fusion.306
  78.6 1.0 fusion.306
  82.1 6.4 collective-permute-done.2
  89.3 1.4 collective-permute-done.3
  91.1 60.0 %while.68 = (s32[]{:T(128)}, f32[3,80,64]{1,2,0:T(8,128)S(1)}, s32[12,16]{1,0:T(8,128)S(1)}, f32[2,80,64]{1,2,0:T(8,128)S(1)}, s32[12,16]{1,0:T(8,128)S(1)}, /*i...) while((s32[]{:T(128)}, f32[3,80,64]{1,2,0:T(8,128)S(1)}, ...), condition=%wide.region_11.12_spmd.clone, body=%wide.region_8.11_spmd.clone.sunk | while | flops 17876564 | bytes 2778059 | solution.py:135
  108.6 1.0 fusion.322
  128.6 1.0 fusion.322
  148.6 1.0 fusion.322
  152.0 6.5 collective-permute-done.4
  159.5 1.4 collective-permute-done.5
  161.3 60.0 %while.69 = (s32[]{:T(128)}, f32[3,80,64]{1,2,0:T(8,128)S(1)}, s32[12,16]{1,0:T(8,128)S(1)}, f32[2,80,64]{1,2,0:T(8,128)S(1)}, s32[12,16]{1,0:T(8,128)S(1)}, /*i...) while((s32[]{:T(128)}, f32[3,80,64]{1,2,0:T(8,128)S(1)}, ...), condition=%wide.region_15.16_spmd.clone, body=%wide.region_12.15_spmd.clone.sunk | while | flops 17876564 | bytes 2778059 | solution.py:135
  168.8 1.0 fusion.338
  188.8 1.0 fusion.338
  208.8 1.0 fusion.338
  222.2 6.5 collective-permute-done.6
  229.5 1.4 collective-permute-done.7
  231.3 60.0 %while.70 = (s32[]{:T(128)}, f32[3,80,64]{1,2,0:T(8,128)S(1)}, s32[12,16]{1,0:T(8,128)S(1)}, f32[2,80,64]{1,2,0:T(8,128)S(1)}, s32[12,16]{1,0:T(8,128)S(1)}, /*i...) while((s32[]{:T(128)}, f32[3,80,64]{1,2,0:T(8,128)S(1)}, ...), condition=%wide.region_19.20_spmd.clone, body=%wide.region_16.19_spmd.clone.sunk | while | flops 17876564 | bytes 2778059 | solution.py:135
  292.1 6.5 collective-permute-done.8
  299.4 1.4 collective-permute-done.9
  301.2 77.0 %while.71 = (s32[]{:T(128)}, f32[3,80,64]{1,2,0:T(8,128)S(1)}, f32[]{:T(128)}, s32[12,16]{1,0:T(8,128)S(1)}, f32[2,80,64]{1,2,0:T(8,128)S(1)}, /*index=5*/s32[12...) while((s32[]{:T(128)}, f32[3,80,64]{1,2,0:T(8,128)S(1)}, ...), condition=%wide.region_24.25_spmd.clone, body=%wide.region_20.24_spmd.clone.sunk | while | flops 18283088 | bytes 2786435 | solution.py:135
  303.7 1.8 select_reduce_fusion.3
  310.1 1.8 select_reduce_fusion.3
  316.5 1.8 select_reduce_fusion.3
  323.0 1.8 select_reduce_fusion.3
  329.4 1.8 select_reduce_fusion.3
  335.8 1.8 select_reduce_fusion.3
  342.2 1.8 select_reduce_fusion.3
  348.6 1.8 select_reduce_fusion.3
  355.0 1.8 select_reduce_fusion.3
  361.5 1.8 select_reduce_fusion.3
  367.9 1.8 select_reduce_fusion.3
  374.3 1.8 select_reduce_fusion.3
  380.1 5.7 collective-permute-done.10
  391.2 10.9 %psum.7 = f32[]{:T(128)} all-reduce(f32[]{:T(128)} %get-tuple-element.598), channel_id=1, replica_groups=mesh['rep'=64,'slab'=4] {'slab'}, use_global_device_ids=true, to_apply=%region_26.27 | all-reduce | flops 1 | bytes 8 | tf_op jit(solution)/shard_map/psum | solution.py:150
  402.8 359.3 %all-gather.4.cloned.1.call-done = f32[64,6,4096]{2,1,0:T(8,128)} async-done(((f32[1,6,4096]{2,1,0:T(8,128)}), f32[64,6,4096]{2,1,0:T(8,128)}) %all-gather.4.cloned.1.call-update) | async-done | bytes 6291472 | tf_op jit(solution)/shard_map/all_gather | solution.py:154
  762.1 4.5 select_reduce_fusion.1
  (1011 shorter events, 287.0 us)
Async XLA Ops:
  7.2 754.9 %all-gather.4.cloned.1.call-start = ((), (), s32[]{:S(2)}) async-start(), calls=%async_computation | async-start | bytes 8519680 | tf_op jit(solution)/shard_map/all_gather | solution.py:154
  9.7 10.2 %collective-permute-start = (f32[2,1024]{1,0:T(2,128)S(1)}, f32[2,1024]{1,0:T(2,128)S(1)}, u32[]{:S(2)}, u32[]{:S(2)}) collective-permute-start(f32[2,1024]{1,0:T(2,128)S(1)} %reshape.1061), channel_id=1, source_target_pairs={{0,3},{1,0},{2,1},{3,2},{4,7},{5,4},{6,5},{7,6},{8,11},{9,8},{10,9... | collective-permute-start | bytes 24584 | tf_op jit(solution)/shard_map/ppermute | solution.py:22
  16.6 3.5 collective-permute-start.1
  21.1 60.4 %copy-start.3 = (f32[4096]{0:T(1024)S(1)}, f32[4096]{0:T(1024)}, u32[]{:S(2)}) copy-start(f32[4096]{0:T(1024)} %param.23) | copy-start | bytes 49156
  21.1 60.7 %copy-start.1 = (f32[1,3,4096]{2,0,1:T(1,128)S(1)}, f32[1,3,4096]{2,0,1:T(1,128)}, u32[]{:S(2)}) copy-start(f32[1,3,4096]{2,0,1:T(1,128)} %param.22) | copy-start | bytes 147460
  21.1 67.5 %copy-start.2 = (s32[1,16]{1,0:T(1,128)S(1)}, s32[1,16]{1,0:T(1,128)}, u32[]{:S(2)}) copy-start(s32[1,16]{1,0:T(1,128)} %param.29) | copy-start | bytes 196
  81.2 9.6 %copy-start.4 = (f32[3]{0:T(128)S(1)}, f32[3]{0:T(128)}, u32[]{:S(2)}) copy-start(f32[3]{0:T(128)} %constant.233.clone) | copy-start | bytes 40
  81.5 7.1 collective-permute-start.2
  89.3 1.5 collective-permute-start.3
  151.4 7.1 collective-permute-start.4
  159.3 1.7 collective-permute-start.5
  221.6 7.1 collective-permute-start.6
  229.4 1.5 collective-permute-start.7
  291.5 7.1 collective-permute-start.8
  299.4 1.5 collective-permute-start.9
  378.2 8.2 %copy-start = (f32[1,3,4096]{2,0,1:T(1,128)S(1)}, f32[1,3,4096]{2,0,1:T(1,128)}, u32[]{:S(2)}) copy-start(f32[1,3,4096]{2,0,1:T(1,128)} %param.21) | copy-start | bytes 147460
  378.4 8.9 %copy-start.5 = (s32[16,2]{0,1:T(2,128)S(1)}, s32[16,2]{0,1:T(2,128)}, u32[]{:S(2)}) copy-start(s32[16,2]{0,1:T(2,128)} %param.30) | copy-start | bytes 388
  378.5 7.3 collective-permute-start.10
Sparse Core Ops, SparseCore 0:
  387.4 374.6 all-gather.3
where the time goes:
time: 778 us; the launch traced here: 776 us
  waiting for transfers between devices  397 us (51%)
  other arithmetic  204 us (26%)
  matrix products  91.9 us (12%)
  local copies, waits for them, and re-layouts  31.6 us (4%)
  between operations  18.9 us (2%)
  loops' own time  12.9 us (2%)
  blocking collectives  10.9 us (1%)
  starting transfers between devices  8.55 us (1%)
    all_gather x1, waiting for transfers between devices, local(): shard_rows = lax.all_gather(state[None], 'rep', axis=0, tiled=True)  359 us
    mul x108, other arithmetic, pair_block(): pushes = (2.0 * slope * weight_col)[None, :, :] * offsets  89 us
    reduce_sum x60, other arithmetic, pair_block(): force_j = -pushes.sum(1).reshape(3, count_tiles, CL)  56.1 us
    ppermute x11, waiting for transfers between devices, from_behind(): return lax.ppermute(value, axis, pairs)  37.5 us
    sub x60, other arithmetic, pair_block(): coords_i[:, :, :, None] - coords_j[:, None, :, :]  28.5 us
    reduce_sum x12, other arithmetic, pair_block(): jnp.sum(jnp.where(self_pair, 0.0, (gauss_term + coulomb) * weight_col))  21.4 us
    dot_general x60, matrix products, pair_block(): jnp.einsum('te,xtc->xec', select_second, force_j, precision=exact)  18.1 us
    dot_general x60, matrix products, pair_block(): jnp.einsum('te,xec->xtc', select_second, extended, precision=exact)  17.7 us
  transfers between devices with their start and end apart: 12, of which 10 were waited for; matrix products, arithmetic and copies ran while one was open for 1% of the time, Pallas kernels for 0%

commit v1 on v0

--- a/solution.py
+++ b/solution.py
@@ -151,7 +151,9 @@
     potential = (total_energy / (atoms_here * lax.axis_size("slab"))).reshape(1)
     state = jnp.concatenate([coords, speeds], 0)
     partner_me = partner_of(swap_pairs, lax.axis_index("rep").reshape(1))[0]
-    shard_rows = lax.all_gather(state[None], "rep", axis=0, tiled=True)
+    shard_rows = jnp.concatenate(
+        lax.all_to_all(jnp.stack([state[None]] * lax.axis_size("rep")), "rep", 0, 0), axis=0
+    )
     row_ids = jnp.arange(shard_rows.shape[0], dtype=jnp.int32)
     chosen = row_ids == partner_me
     swapped = jnp.sum(jnp.where(chosen[:, None, None], shard_rows, 0.0), 0)

time: 778 us -> 547 us (0.70)
  waiting for transfers between devices: 397 us -> 69.8 us
  blocking collectives: 10.9 us -> 101 us
  between operations: 18.9 us -> 5.55 us
  starting transfers between devices: 8.55 us -> 18.2 us
  other arithmetic: 204 us -> 212 us
    all_gather x1 -> x0, waiting for transfers between devices: 359 us -> none  [local(): shard_rows = lax.all_gather(state[None], 'rep', axis=0, tiled=True)]
    psum x1, blocking collectives: 10.9 us -> 101 us  [local(): total_energy = lax.psum(energy, 'slab')]
    all_to_all x0 -> x1, waiting for transfers between devices: none -> 32.4 us  [local(): lax.all_to_all(jnp.stack([state[None]] * lax.axis_size('rep')), 'rep', 0, 0)]
    all_to_all x0 -> x1, starting transfers between devices: none -> 9.64 us  [local(): lax.all_to_all(jnp.stack([state[None]] * lax.axis_size('rep')), 'rep', 0, 0)]
where the time goes in v1:
time: 547 us; the launch traced here: 544 us
  other arithmetic  212 us (39%)
  blocking collectives  101 us (18%)
  matrix products  85.9 us (16%)
  waiting for transfers between devices  69.8 us (13%)
  local copies, waits for them, and re-layouts  38.3 us (7%)
  starting transfers between devices  18.2 us (3%)
  loops' own time  13.2 us (2%)
  between operations  5.55 us (1%)
    psum x1, blocking collectives, local(): total_energy = lax.psum(energy, 'slab')  101 us
    mul x108, other arithmetic, pair_block(): pushes = (2.0 * slope * weight_col)[None, :, :] * offsets  91.2 us
    reduce_sum x60, other arithmetic, pair_block(): force_j = -pushes.sum(1).reshape(3, count_tiles, CL)  56.2 us
    ppermute x11, waiting for transfers between devices, from_behind(): return lax.ppermute(value, axis, pairs)  37.4 us
    all_to_all x1, waiting for transfers between devices, local(): lax.all_to_all(jnp.stack([state[None]] * lax.axis_size('rep')), 'rep', 0, 0)  32.4 us
    sub x60, other arithmetic, pair_block(): coords_i[:, :, :, None] - coords_j[:, None, :, :]  29.5 us
    reduce_sum x12, other arithmetic, pair_block(): jnp.sum(jnp.where(self_pair, 0.0, (gauss_term + coulomb) * weight_col))  21.4 us
    dot_general x60, matrix products, pair_block(): jnp.einsum('te,xtc->xec', select_second, force_j, precision=exact)  18 us
  transfers between devices with their start and end apart: 12, of which 10 were waited for; matrix products, arithmetic and copies ran while one was open for 1% of the time, Pallas kernels for 0%

profile of v1, /device:TPU:0, one launch (start us, length us, event | category | flops | bytes accessed | tf_op | source)
XLA Modules:
  0.0 544.4 jit_solution(176474316247181587)
XLA Ops:
  3.1 4.9 collective-permute-start
  14.6 60.1 %while.67 = (s32[]{:T(128)}, f32[3,80,64]{1,2,0:T(8,128)S(1)}, s32[12,16]{1,0:T(8,128)S(1)}, f32[2,80,64]{1,2,0:T(8,128)S(1)}, s32[12,16]{1,0:T(8,128)S(1)}, /*i...) while((s32[]{:T(128)}, f32[3,80,64]{1,2,0:T(8,128)S(1)}, ...), condition=%wide.region_7.8_spmd.clone, body=%wide.region_4.7_spmd.clone.sunk | while | flops 17876564 | bytes 2778051 | solution.py:135
  17.0 1.1 fusion.307
  22.0 1.1 fusion.307
  27.0 1.1 fusion.307
  32.0 1.1 fusion.307
  37.0 1.1 fusion.307
  42.0 1.1 fusion.307
  47.0 1.1 fusion.307
  52.0 1.1 fusion.307
  57.1 1.1 fusion.307
  62.1 1.1 fusion.307
  67.1 1.1 fusion.307
  72.1 1.1 fusion.307
  75.6 6.4 %collective-permute-done.2 = f32[3,1024]{1,0:T(4,128)S(1)} collective-permute-done((f32[3,1024]{1,0:T(4,128)S(1)}, f32[3,1024]{1,0:T(4,128)S(1)}, u32[]{:S(2)}, u32[]{:S(2)}) %collective-permute-start.2) | collective-permute-done | bytes 12320 | tf_op jit(solution)/shard_map/ppermute | solution.py:22
  82.8 1.4 collective-permute-done.3
  84.6 60.1 %while.68 = (s32[]{:T(128)}, f32[3,80,64]{1,2,0:T(8,128)S(1)}, s32[12,16]{1,0:T(8,128)S(1)}, f32[2,80,64]{1,2,0:T(8,128)S(1)}, s32[12,16]{1,0:T(8,128)S(1)}, /*i...) while((s32[]{:T(128)}, f32[3,80,64]{1,2,0:T(8,128)S(1)}, ...), condition=%wide.region_11.12_spmd.clone, body=%wide.region_8.11_spmd.clone.sunk | while | flops 17876564 | bytes 2778051 | solution.py:135
  92.1 1.1 fusion.323
  97.1 1.1 fusion.323
  107.1 1.1 fusion.323
  112.1 1.1 fusion.323
  145.5 6.5 %collective-permute-done.4 = f32[3,1024]{1,0:T(4,128)S(1)} collective-permute-done((f32[3,1024]{1,0:T(4,128)S(1)}, f32[3,1024]{1,0:T(4,128)S(1)}, u32[]{:S(2)}, u32[]{:S(2)}) %collective-permute-start.4) | collective-permute-done | bytes 12320 | tf_op jit(solution)/shard_map/ppermute | solution.py:22
  153.0 1.4 collective-permute-done.5
  154.8 60.1 %while.69 = (s32[]{:T(128)}, f32[3,80,64]{1,2,0:T(8,128)S(1)}, s32[12,16]{1,0:T(8,128)S(1)}, f32[2,80,64]{1,2,0:T(8,128)S(1)}, s32[12,16]{1,0:T(8,128)S(1)}, /*i...) while((s32[]{:T(128)}, f32[3,80,64]{1,2,0:T(8,128)S(1)}, ...), condition=%wide.region_15.16_spmd.clone, body=%wide.region_12.15_spmd.clone.sunk | while | flops 17876564 | bytes 2778051 | solution.py:135
  215.8 6.5 %collective-permute-done.6 = f32[3,1024]{1,0:T(4,128)S(1)} collective-permute-done((f32[3,1024]{1,0:T(4,128)S(1)}, f32[3,1024]{1,0:T(4,128)S(1)}, u32[]{:S(2)}, u32[]{:S(2)}) %collective-permute-start.6) | collective-permute-done | bytes 12320 | tf_op jit(solution)/shard_map/ppermute | solution.py:22
  223.1 1.4 collective-permute-done.7
  224.9 60.1 %while.70 = (s32[]{:T(128)}, f32[3,80,64]{1,2,0:T(8,128)S(1)}, s32[12,16]{1,0:T(8,128)S(1)}, f32[2,80,64]{1,2,0:T(8,128)S(1)}, s32[12,16]{1,0:T(8,128)S(1)}, /*i...) while((s32[]{:T(128)}, f32[3,80,64]{1,2,0:T(8,128)S(1)}, ...), condition=%wide.region_19.20_spmd.clone, body=%wide.region_16.19_spmd.clone.sunk | while | flops 17876564 | bytes 2778051 | solution.py:135
  285.8 6.5 %collective-permute-done.8 = f32[3,1024]{1,0:T(4,128)S(1)} collective-permute-done((f32[3,1024]{1,0:T(4,128)S(1)}, f32[3,1024]{1,0:T(4,128)S(1)}, u32[]{:S(2)}, u32[]{:S(2)}) %collective-permute-start.8) | collective-permute-done | bytes 12320 | tf_op jit(solution)/shard_map/ppermute | solution.py:22
  293.1 1.4 collective-permute-done.9
  294.9 77.1 %while.71 = (s32[]{:T(128)}, f32[3,80,64]{1,2,0:T(8,128)S(1)}, f32[]{:T(128)}, s32[12,16]{1,0:T(8,128)S(1)}, f32[2,80,64]{1,2,0:T(8,128)S(1)}, /*index=5*/s32[12...) while((s32[]{:T(128)}, f32[3,80,64]{1,2,0:T(8,128)S(1)}, ...), condition=%wide.region_24.25_spmd.clone, body=%wide.region_20.24_spmd.clone.sunk | while | flops 18283088 | bytes 2786427 | solution.py:135
  297.4 1.8 select_reduce_fusion.2
  303.8 1.8 select_reduce_fusion.2
  310.2 1.8 select_reduce_fusion.2
  316.6 1.8 select_reduce_fusion.2
  323.1 1.8 select_reduce_fusion.2
  329.5 1.8 select_reduce_fusion.2
  335.9 1.8 select_reduce_fusion.2
  342.3 1.8 select_reduce_fusion.2
  348.8 1.8 select_reduce_fusion.2
  355.2 1.8 select_reduce_fusion.2
  361.6 1.8 select_reduce_fusion.2
  368.0 1.8 select_reduce_fusion.2
  373.9 5.7 %collective-permute-done.10 = f32[3,1024]{1,0:T(4,128)S(1)} collective-permute-done((f32[3,1024]{1,0:T(4,128)S(1)}, f32[3,1024]{1,0:T(4,128)S(1)}, u32[]{:S(2)}, u32[]{:S(2)}) %collective-permute-start.10) | collective-permute-done | bytes 12320 | tf_op jit(solution)/shard_map/ppermute | solution.py:22
  380.4 4.4 stack.69
  384.8 9.6 %all-to-all-start = ((f32[64,1,6,4096]{3,1,2,0:T(1,128)}), f32[64,1,6,4096]{3,1,2,0:T(1,128)}, u32[]{:S(2)}, u32[]{:S(2)}) async-start(f32[64,1,6,4096]{3,1,2,0:T(1,128)} %stack.69), calls=%async_computation | async-start | bytes 12582912 | tf_op jit(solution)/shard_map/all_to_all | solution.py:155
  398.3 101.5 %psum.7 = f32[]{:T(128)} all-reduce(f32[]{:T(128)} %get-tuple-element.598), channel_id=1, replica_groups=mesh['rep'=64,'slab'=4] {'slab'}, use_global_device_ids=true, to_apply=%region_26.27 | all-reduce | flops 1 | bytes 8 | tf_op jit(solution)/shard_map/psum | solution.py:150
  500.5 32.4 %all-to-all-done = f32[64,1,6,4096]{3,1,2,0:T(1,128)} async-done(((f32[64,1,6,4096]{3,1,2,0:T(1,128)}), f32[64,1,6,4096]{3,1,2,0:T(1,128)}, u32[]{:S(2)}, u32[]{:S(2)}) %all-to-all-start) | async-done | bytes 6291488 | tf_op jit(solution)/shard_map/all_to_all | solution.py:155
  532.8 9.1 %fusion.130 = f32[6,4096]{1,0:T(8,128)S(1)} fusion(f32[64,1,6,4096]{3,1,2,0:T(1,128)} %all-to-all-done, pred[64]{0:T(512)(128)(4,1)S(1)} %iota_compare_fusion.12), kind=kLoop, calls=%fused_computation.232 | loop fusion | flops 3121152 | bytes 6389824 | tf_op jit(solution)/shard_map/reduce_sum | solution.py:159
  (1011 shorter events, 287.7 us)
Async XLA Ops:
  3.1 10.2 %collective-permute-start = (f32[2,1024]{1,0:T(2,128)S(1)}, f32[2,1024]{1,0:T(2,128)S(1)}, u32[]{:S(2)}, u32[]{:S(2)}) collective-permute-start(f32[2,1024]{1,0:T(2,128)S(1)} %reshape.1066), channel_id=1, source_target_pairs={{0,3},{1,0},{2,1},{3,2},{4,7},{5,4},{6,5},{7,6},{8,11},{9,8},{10,9... | collective-permute-start | bytes 24584 | tf_op jit(solution)/shard_map/ppermute | solution.py:22
  10.1 3.5 collective-permute-start.1
  14.5 60.5 %copy-start.3 = (f32[4096]{0:T(1024)S(1)}, f32[4096]{0:T(1024)}, u32[]{:S(2)}) copy-start(f32[4096]{0:T(1024)} %param.23) | copy-start | bytes 49156
  14.5 60.7 %copy-start.1 = (f32[1,3,4096]{2,0,1:T(1,128)S(1)}, f32[1,3,4096]{2,0,1:T(1,128)}, u32[]{:S(2)}) copy-start(f32[1,3,4096]{2,0,1:T(1,128)} %param.22) | copy-start | bytes 147460
  14.5 67.6 %copy-start.2 = (s32[1,16]{1,0:T(1,128)S(1)}, s32[1,16]{1,0:T(1,128)}, u32[]{:S(2)}) copy-start(s32[1,16]{1,0:T(1,128)} %param.29) | copy-start | bytes 196
  74.7 9.6 %copy-start.4 = (f32[3]{0:T(128)S(1)}, f32[3]{0:T(128)}, u32[]{:S(2)}) copy-start(f32[3]{0:T(128)} %constant.233.clone) | copy-start | bytes 40
  74.9 7.1 %collective-permute-start.2 = (f32[3,1024]{1,0:T(4,128)S(1)}, f32[3,1024]{1,0:T(4,128)S(1)}, u32[]{:S(2)}, u32[]{:S(2)}) collective-permute-start(f32[3,1024]{1,0:T(4,128)S(1)} %reshape.1072), channel_id=1, source_target_pairs={{0,1},{1,2},{2,3},{3,0},{4,5},{5,6},{6,7},{7,4},{8,9},{9,10},{10,1... | collective-permute-start | bytes 36872 | tf_op jit(solution)/shard_map/ppermute | solution.py:22
  82.8 1.5 collective-permute-start.3
  145.0 7.1 %collective-permute-start.4 = (f32[3,1024]{1,0:T(4,128)S(1)}, f32[3,1024]{1,0:T(4,128)S(1)}, u32[]{:S(2)}, u32[]{:S(2)}) collective-permute-start(f32[3,1024]{1,0:T(4,128)S(1)} %reshape.1077), channel_id=1, source_target_pairs={{0,1},{1,2},{2,3},{3,0},{4,5},{5,6},{6,7},{7,4},{8,9},{9,10},{10,1... | collective-permute-start | bytes 36872 | tf_op jit(solution)/shard_map/ppermute | solution.py:22
  152.8 1.7 collective-permute-start.5
  215.2 7.1 %collective-permute-start.6 = (f32[3,1024]{1,0:T(4,128)S(1)}, f32[3,1024]{1,0:T(4,128)S(1)}, u32[]{:S(2)}, u32[]{:S(2)}) collective-permute-start(f32[3,1024]{1,0:T(4,128)S(1)} %reshape.1082), channel_id=1, source_target_pairs={{0,1},{1,2},{2,3},{3,0},{4,5},{5,6},{6,7},{7,4},{8,9},{9,10},{10,1... | collective-permute-start | bytes 36872 | tf_op jit(solution)/shard_map/ppermute | solution.py:22
  223.0 1.5 collective-permute-start.7
  285.2 7.1 %collective-permute-start.8 = (f32[3,1024]{1,0:T(4,128)S(1)}, f32[3,1024]{1,0:T(4,128)S(1)}, u32[]{:S(2)}, u32[]{:S(2)}) collective-permute-start(f32[3,1024]{1,0:T(4,128)S(1)} %reshape.1087), channel_id=1, source_target_pairs={{0,1},{1,2},{2,3},{3,0},{4,5},{5,6},{6,7},{7,4},{8,9},{9,10},{10,1... | collective-permute-start | bytes 36872 | tf_op jit(solution)/shard_map/ppermute | solution.py:22
  293.0 1.5 collective-permute-start.9
  372.0 8.2 %copy-start = (f32[1,3,4096]{2,0,1:T(1,128)S(1)}, f32[1,3,4096]{2,0,1:T(1,128)}, u32[]{:S(2)}) copy-start(f32[1,3,4096]{2,0,1:T(1,128)} %param.21) | copy-start | bytes 147460
  372.3 7.3 %collective-permute-start.10 = (f32[3,1024]{1,0:T(4,128)S(1)}, f32[3,1024]{1,0:T(4,128)S(1)}, u32[]{:S(2)}, u32[]{:S(2)}) collective-permute-start(f32[3,1024]{1,0:T(4,128)S(1)} %reshape.1092), channel_id=1, source_target_pairs={{0,1},{1,2},{2,3},{3,0},{4,5},{5,6},{6,7},{7,4},{8,9},{9,10},{10,1... | collective-permute-start | bytes 36872 | tf_op jit(solution)/shard_map/ppermute | solution.py:22
  384.8 9.7 %copy-start.5 = (s32[16,2]{0,1:T(2,128)S(1)}, s32[16,2]{0,1:T(2,128)}, u32[]{:S(2)}) copy-start(s32[16,2]{0,1:T(2,128)} %param.30) | copy-start | bytes 388
  384.8 148.1 %all-to-all-start = ((f32[64,1,6,4096]{3,1,2,0:T(1,128)}), f32[64,1,6,4096]{3,1,2,0:T(1,128)}, u32[]{:S(2)}, u32[]{:S(2)}) async-start(f32[64,1,6,4096]{3,1,2,0:T(1,128)} %stack.69), calls=%async_computation | async-start | bytes 12582912 | tf_op jit(solution)/shard_map/all_to_all | solution.py:155
